TPU v7x, 32 devices: a whole 2x2x4 slice. The times are simulated.
32 devices in a mesh: dp: 2 (over y), row: 4 (over x, core), col: 4 (over z).
Axes of the slice: x: 2, y: 2, z: 4, core: 2. Of those that a mesh axis runs over, the one named last changes fastest.
Arguments:
- patches: bfloat16 [2, 512, 1456], P('dp', 'col', 'row'), may hold values from -6 to 6
- queries: bfloat16 [2, 512, 6144], P('dp', 'col', 'row'), may hold values from -6 to 6
- attn_keys: bfloat16 [2, 512, 6144], P('dp', 'col', 'row'), may hold values from -6 to 6
- attn_values: bfloat16 [2, 512, 6144], P('dp', 'col', 'row'), may hold values from -6 to 6
- out_weight: bfloat16 [6144, 12288], P('row', 'col'), may hold values from -0.15625 to 0.15625
- output_grad: bfloat16 [2, 512, 12288], P('dp', 'row', 'col'), may hold values from -4 to 4
Outputs:
- query_grad: float32 [2, 512, 6144], P('dp', 'col', 'row')
- key_grad: float32 [2, 512, 6144], P('dp', 'col', 'row')
- value_grad: float32 [2, 512, 6144], P('dp', 'col', 'row')
- out_weight_grad: float32 [6144, 12288], P('row', 'col')
- embed_weight_grad: float32 [1456, 12288], P('row', 'col')
All inputs are finite; a program needn't handle non-finite values.
Results may differ from a plain program's by a relative error of at most 0.025.
Values may be sent and summed in bfloat16 or wider, within the bound.
No kernel may reach another device: no remote copies, remote signals or barrier semaphores. Data moves between devices by JAX's collectives and lax.ppermute only.
A program may use at most 128 MiB of HBM per device.

v0:
```python
import jax
import jax.numpy as jnp
from jax import lax
from jax.sharding import PartitionSpec as P

DH = 128


def contract_rows(left, right):
    return lax.dot_general(
        left, right, (((0,), (0,)), ((), ())), preferred_element_type=jnp.float32
    )


def swap_dp(x):
    return lax.ppermute(x, "dp", [(0, 1), (1, 0)])


def body(patches, queries, attn_keys, attn_values, out_weight, output_grad):
    factor = DH ** (-0.5)
    local_rows = queries.shape[1]
    feature_width = queries.shape[2]
    head_count = feature_width // DH
    grad_other = swap_dp(output_grad)
    patch_other = swap_dp(lax.all_gather(patches, "col", axis=1, tiled=True))
    every_key, every_value, every_patch = (
        lax.all_gather(attn_keys, "col", axis=1, tiled=True),
        lax.all_gather(attn_values, "col", axis=1, tiled=True),
        lax.all_gather(patches, "col", axis=1, tiled=True),
    )
    local_query = queries[0].reshape(local_rows, head_count, DH)
    all_keys = every_key[0].reshape(-1, head_count, DH)
    all_values = every_value[0].reshape(-1, head_count, DH)
    scores = (
        jnp.einsum("qhd,khd->hqk", local_query, all_keys, preferred_element_type=jnp.float32)
        * factor
    )
    row_max = jnp.max(scores, axis=2, keepdims=True)
    log_total = row_max + jnp.log(jnp.sum(jnp.exp(scores - row_max), axis=2, keepdims=True))
    attn_probs = jnp.exp(scores - log_total).astype(jnp.bfloat16)
    attn_out = jnp.einsum(
        "hqk,khd->qhd", attn_probs, all_values, preferred_element_type=jnp.float32
    ).astype(jnp.bfloat16)
    out_local = attn_out.reshape(1, local_rows, feature_width)
    dense_grad = lax.all_gather(output_grad, "row", axis=1, tiled=True)[0]
    attn_grad = lax.psum_scatter(
        lax.dot_general(
            dense_grad, out_weight, (((1,), (1,)), ((), ())), preferred_element_type=jnp.float32
        ),
        "col",
        scatter_dimension=0,
        tiled=True,
    ).astype(jnp.bfloat16)
    grad_heads = attn_grad.reshape(local_rows, head_count, DH)
    prob_grad = jnp.einsum(
        "qhd,khd->hqk", grad_heads, all_values, preferred_element_type=jnp.float32
    )
    row_dot = jnp.transpose(
        jnp.sum(grad_heads.astype(jnp.float32) * attn_out.astype(jnp.float32), axis=2)
    )[:, :, None]
    score_grad = (attn_probs.astype(jnp.float32) * (prob_grad - row_dot)).astype(jnp.bfloat16)
    query_grad = (
        jnp.einsum("hqk,khd->qhd", score_grad, all_keys, preferred_element_type=jnp.float32)
        * factor
    )
    every_out = lax.all_gather(out_local, "col", axis=1, tiled=True)
    key_term = (
        jnp.einsum("hqk,qhd->khd", score_grad, local_query, preferred_element_type=jnp.float32)
        * factor
    )
    value_term = jnp.einsum(
        "hqk,qhd->khd", attn_probs, grad_heads, preferred_element_type=jnp.float32
    )
    key_sum, value_sum = (
        lax.psum_scatter(
            key_term.reshape(-1, feature_width).astype(jnp.bfloat16),
            "col",
            scatter_dimension=0,
            tiled=True,
        ).astype(jnp.float32),
        lax.psum_scatter(
            value_term.reshape(-1, feature_width).astype(jnp.bfloat16),
            "col",
            scatter_dimension=0,
            tiled=True,
        ).astype(jnp.float32),
    )
    out_pair = jnp.concatenate([every_out, swap_dp(every_out)], axis=0)
    grad_pair = lax.all_gather(
        jnp.concatenate([output_grad, grad_other], axis=0), "row", axis=1, tiled=True
    )
    patch_pair = jnp.concatenate([every_patch, patch_other], axis=0)
    out_weight_grad = lax.dot_general(
        out_pair, grad_pair, (((0, 1), (0, 1)), ((), ())), preferred_element_type=jnp.float32
    )
    embed_weight_grad = lax.dot_general(
        patch_pair, grad_pair, (((0, 1), (0, 1)), ((), ())), preferred_element_type=jnp.float32
    )
    return (
        query_grad.reshape(1, local_rows, feature_width),
        key_sum.reshape(1, local_rows, feature_width),
        value_sum.reshape(1, local_rows, feature_width),
        out_weight_grad,
        embed_weight_grad,
    )


def solution(mesh):
    placed = (
        P("dp", "col", "row"),
        P("dp", "col", "row"),
        P("dp", "col", "row"),
        P("dp", "col", "row"),
        P("row", "col"),
        P("dp", "row", "col"),
    )
    return jax.shard_map(
        body,
        mesh=mesh,
        in_specs=placed,
        out_specs=(
            P("dp", "col", "row"),
            P("dp", "col", "row"),
            P("dp", "col", "row"),
            P("row", "col"),
            P("row", "col"),
        ),
        check_vma=False,
    )
```

profile of v0, /device:TPU:0, one launch (start us, length us, event | category | flops | bytes accessed | tf_op | source)
XLA Modules:
  0.0 366.7 jit_solution(11999108349264509849)
XLA Ops:
  7.9 1.9 copy.22
  9.9 30.9 %all-gather.8.cloned.1.call-done = bf16[1,512,3072]{2,1,0:T(8,128)(2,1)} async-done(((bf16[1,128,3072]{2,1,0:T(8,128)(2,1)}), bf16[1,512,3072]{2,1,0:T(8,128)(2,1)}) %all-gather.8.cloned.1.call-update) | async-done | bytes 3145744 | tf_op jit(solution)/shard_map/all_gather | solution.py:45
  40.8 10.6 %fusion.3 = f32[512,1536]{1,0:T(8,128)} fusion(bf16[1536,3072]{1,0:T(8,128)(2,1)} %param.10, bf16[1,512,3072]{2,1,0:T(8,128)(2,1)} %all-gather.8.cloned.1.call-done), kind=kOutput, calls=%fused_computation.5 | convolution fusion | flops 4831838208 | bytes 15728640 | tf_op jit(solution)/shard_map/dot_general | solution.py:47
  53.7 27.0 %all-gather.6.cloned.1.call-done = bf16[1,512,1536]{1,2,0:T(8,128)(2,1)} async-done(((bf16[1,128,1536]{1,2,0:T(8,128)(2,1)}), bf16[1,512,1536]{1,2,0:T(8,128)(2,1)}) %all-gather.6.cloned.1.call-update) | async-done | bytes 1572880 | tf_op jit(solution)/shard_map/all_gather | solution.py:27
  80.7 2.1 multiply_reduce_fusion
  84.4 57.7 %reduce-scatter.4.cloned.1.call-done = f32[128,1536]{1,0:T(8,128)} async-done(((f32[512,1536]{1,0:T(8,128)}), f32[128,1536]{1,0:T(8,128)}) %reduce-scatter.4.cloned.1.call-update) | async-done | bytes 786448 | tf_op jit(solution)/shard_map/reduce_scatter | solution.py:46
  143.5 38.4 %all-gather.10.cloned.1.call-done = bf16[1,512,1536]{1,2,0:T(8,128)(2,1)} async-done(((bf16[1,128,1536]{1,2,0:T(8,128)(2,1)}), bf16[1,512,1536]{1,2,0:T(8,128)(2,1)}) %all-gather.10.cloned.1.call-update) | async-done | bytes 1572880 | tf_op jit(solution)/shard_map/all_gather | solution.py:28
  181.9 2.7 multiply_reduce_fusion.1
  186.3 17.8 %collective-permute-done.1 = bf16[1,128,3072]{2,1,0:T(8,128)(2,1)S(1)} collective-permute-done((bf16[1,128,3072]{2,1,0:T(8,128)(2,1)S(1)}, bf16[1,128,3072]{2,1,0:T(8,128)(2,1)S(1)}, u32[]{:S(2)}, u32[]{:S(2)}) %collective-permute-start.1) | collective-permute-done | bytes 786464 | tf_op jit(solution)/shard_map/ppermute | solution.py:16
  205.4 2.0 multiply_convert_fusion.1
  207.5 2.7 multiply_convert_fusion
  210.2 2.6 copy.29
  212.8 1.7 convolution_convert_fusion
  214.5 2.6 copy.30
  217.2 14.4 %all_gather.24 = bf16[1,512,364]{1,2,0:T(8,128)(2,1)S(1)} all-gather(bf16[1,128,364]{1,2,0:T(8,128)(2,1)S(1)} %copy-done.5), channel_id=1, replica_groups=mesh['dp'=2,'row'=4,'col'=4] {'col'}, dimensions={1}, use_global_device_ids=true | all-gather | bytes 465920 | tf_op jit(solution)/shard_map/all_gather | solution.py:29
  233.6 9.8 %collective-permute-done.2 = bf16[1,512,364]{1,2,0:T(8,128)(2,1)} collective-permute-done((bf16[1,512,364]{1,2,0:T(8,128)(2,1)S(1)}, bf16[1,512,364]{1,2,0:T(8,128)(2,1)}, u32[]{:S(2)}, u32[]{:S(2)}) %collective-permute-start.2) | collective-permute-done | bytes 372768 | tf_op jit(solution)/shard_map/ppermute | solution.py:16
  243.3 23.4 %all-gather.14.cloned.1.call-done = bf16[2,512,3072]{2,1,0:T(8,128)(2,1)} async-done(((bf16[2,128,3072]{2,1,0:T(8,128)(2,1)}), bf16[2,512,3072]{2,1,0:T(8,128)(2,1)}) %all-gather.14.cloned.1.call-update) | async-done | bytes 6291472 | tf_op jit(solution)/shard_map/all_gather | solution.py:89
  266.8 7.5 %convolution_bitcast_fusion.1 = f32[364,3072]{1,0:T(8,128)} fusion(bf16[2,512,3072]{2,1,0:T(8,128)(2,1)} %all-gather.14.cloned.1.call-done, bf16[1,512,364]{1,2,0:T(8,128)(2,1)} %collective-permute-done.2, bf16[1,512,364]{1,2,0:T(8,128)(2,1)S(1)} %all_gather.24), kind=kOutput, calls=%fused_computation.1 | convolution fusion | flops 2290462720 | bytes 11509760 | tf_op jit(solution)/shard_map/dot_general | solution.py:96
  275.8 2.4 copy.31
  278.2 26.8 %reduce-scatter.6.cloned.1.call-done = bf16[128,1536]{1,0:T(8,128)(2,1)} async-done(((bf16[512,1536]{1,0:T(8,128)(2,1)}), bf16[128,1536]{1,0:T(8,128)(2,1)}) %reduce-scatter.6.cloned.1.call-update) | async-done | bytes 393232 | tf_op jit(solution)/shard_map/reduce_scatter | solution.py:75
  305.0 2.0 bitcast_convert_fusion.1
  306.9 34.6 %reduce-scatter.8.cloned.1.call-done = bf16[128,1536]{1,0:T(8,128)(2,1)} async-done(((bf16[512,1536]{1,0:T(8,128)(2,1)}), bf16[128,1536]{1,0:T(8,128)(2,1)}) %reduce-scatter.8.cloned.1.call-update) | async-done | bytes 393232 | tf_op jit(solution)/shard_map/reduce_scatter | solution.py:81
  341.6 2.0 bitcast_convert_fusion
  343.5 16.3 %convolution_bitcast_fusion = f32[1536,3072]{1,0:T(8,128)} fusion(bf16[2,512,3072]{2,1,0:T(8,128)(2,1)} %all-gather.14.cloned.1.call-done, bf16[1,512,1536]{1,2,0:T(8,128)(2,1)} %collective-permute-done, bf16[1,512,1536]{1,2,0:T(8,128)(2,1)S(1)} %copy-done.6), kind=kOutput, calls=%fused_computation | convolution fusion | flops 9665249280 | bytes 28311552 | tf_op jit(solution)/shard_map/dot_general | solution.py:93
  (44 shorter events, 12.5 us)
Async XLA Ops:
  7.2 33.7 %all-gather.8.cloned.1.call-start = ((), (), s32[]{:S(2)}) async-start(), calls=%async_computation.4 | async-start | bytes 3932160 | tf_op jit(solution)/shard_map/all_gather | solution.py:45
  7.9 72.8 %all-gather.6.cloned.1.call-start = ((), (), s32[]{:S(2)}) async-start(), calls=%async_computation.3 | async-start | bytes 1966080 | tf_op jit(solution)/shard_map/all_gather | solution.py:27
  9.9 132.2 %reduce-scatter.4.cloned.1.call-start = ((), (), s32[]{:S(2)}) async-start(), calls=%async_computation.5 | async-start | bytes 3932160 | tf_op jit(solution)/shard_map/reduce_scatter | solution.py:46
  51.4 1.0 copy-start.3
  51.4 2.0 copy-start.4
  51.4 130.4 %all-gather.10.cloned.1.call-start = ((), (), s32[]{:S(2)}) async-start(), calls=%async_computation.6 | async-start | bytes 1966080 | tf_op jit(solution)/shard_map/all_gather | solution.py:28
  53.4 179.4 %all-gather.12.cloned.1.call-start = ((), (), s32[]{:S(2)}) async-start(), calls=%async_computation.9 | async-start | bytes 1966080 | tf_op jit(solution)/shard_map/all_gather | solution.py:66
  53.6 30.2 %copy-start.1 = (bf16[1,128,1536]{1,2,0:T(8,128)(2,1)}, bf16[1,128,1536]{1,2,0:T(8,128)(2,1)S(1)}, u32[]{:S(2)}) copy-start(bf16[1,128,1536]{1,2,0:T(8,128)(2,1)S(1)} %copy.21) | copy-start | bytes 1179652
  84.4 100.3 %copy-start.2 = (bf16[1,128,3072]{2,1,0:T(8,128)(2,1)S(1)}, bf16[1,128,3072]{2,1,0:T(8,128)(2,1)}, u32[]{:S(2)}) copy-start(bf16[1,128,3072]{2,1,0:T(8,128)(2,1)} %param.11) | copy-start | bytes 2359300
  184.6 82.2 %all-gather.14.cloned.1.call-start = ((), (), s32[]{:S(2)}) async-start(), calls=%async_computation.10 | async-start | bytes 7864320 | tf_op jit(solution)/shard_map/all_gather | solution.py:89
  184.7 19.3 %collective-permute-start.1 = (bf16[1,128,3072]{2,1,0:T(8,128)(2,1)S(1)}, bf16[1,128,3072]{2,1,0:T(8,128)(2,1)S(1)}, u32[]{:S(2)}, u32[]{:S(2)}) collective-permute-start(bf16[1,128,3072]{2,1,0:T(8,128)(2,1)S(1)} %copy-done.2), channel_id=1, source_target_pairs={{0,16},{16,0},{1,17},{17,1},{2,18},{18,2},{3,19},{19,3},{4,20},{20... | collective-permute-start | bytes 2359304 | tf_op jit(solution)/shard_map/ppermute | solution.py:16
  205.4 99.6 %reduce-scatter.6.cloned.1.call-start = ((), (), s32[]{:S(2)}) async-start(), calls=%async_computation.7 | async-start | bytes 1966080 | tf_op jit(solution)/shard_map/reduce_scatter | solution.py:75
  212.8 128.8 %reduce-scatter.8.cloned.1.call-start = ((), (), s32[]{:S(2)}) async-start(), calls=%async_computation.8 | async-start | bytes 1966080 | tf_op jit(solution)/shard_map/reduce_scatter | solution.py:81
  214.5 2.6 copy-start.5
  231.5 42.8 %copy-start = (bf16[1,512,1536]{1,2,0:T(8,128)(2,1)S(1)}, bf16[1,512,1536]{1,2,0:T(8,128)(2,1)}, u32[]{:S(2)}) copy-start(bf16[1,512,1536]{1,2,0:T(8,128)(2,1)} %all-gather.6.cloned.1.call-done) | copy-start | bytes 4718596
  231.5 11.8 %collective-permute-start.2 = (bf16[1,512,364]{1,2,0:T(8,128)(2,1)S(1)}, bf16[1,512,364]{1,2,0:T(8,128)(2,1)}, u32[]{:S(2)}, u32[]{:S(2)}) collective-permute-start(bf16[1,512,364]{1,2,0:T(8,128)(2,1)S(1)} %all_gather.24), channel_id=1, source_target_pairs={{0,16},{16,0},{1,17},{17,1},{2,18},{18,2},{3,19},{19,3},{4,20},{20... | collective-permute-start | bytes 1118216 | tf_op jit(solution)/shard_map/ppermute | solution.py:16
  232.7 110.8 %collective-permute-start = (bf16[1,512,1536]{1,2,0:T(8,128)(2,1)}, bf16[1,512,1536]{1,2,0:T(8,128)(2,1)}, u32[]{:S(2)}, u32[]{:S(2)}) collective-permute-start(bf16[1,512,1536]{1,2,0:T(8,128)(2,1)} %all-gather.12.cloned.1.call-done), channel_id=1, source_target_pairs={{0,16},{16,0},{1,17},{17,1},{2,18},{18,2},{3,19},{19,3},{4,20},{20... | collective-permute-start | bytes 4718600 | tf_op jit(solution)/shard_map/ppermute | solution.py:16
  275.8 67.8 %copy-start.6 = (bf16[1,512,1536]{1,2,0:T(8,128)(2,1)S(1)}, bf16[1,512,1536]{1,2,0:T(8,128)(2,1)}, u32[]{:S(2)}) copy-start(bf16[1,512,1536]{1,2,0:T(8,128)(2,1)} %all-gather.12.cloned.1.call-done) | copy-start | bytes 4718596
Sparse Core Ops, SparseCore 0:
  9.6 31.2 all-gather.7
  43.0 37.7 all-gather.5
  83.6 58.4 reduce-scatter.3
  144.1 37.7 all-gather.9
  184.7 35.9 all-gather.11
  222.1 44.5 all-gather.13
  269.6 35.3 reduce-scatter.5
  307.3 34.2 reduce-scatter.7
where the time goes:
time: 367 us
  waiting for transfers between devices  267 us (73%)
  matrix products  47.1 us (13%)
  blocking collectives  14.4 us (4%)
  between operations  14.2 us (4%)
  local copies, waits for them, and re-layouts  11.8 us (3%)
  other arithmetic  7.92 us (2%)
  starting transfers between devices  3.94 us (1%)
    reduce_scatter x1, waiting for transfers between devices, body(): lax.psum_scatter(lax.dot_general(dense_grad, out_weight, (((1,), (1,)), (...  57.7 us
    all_gather x1, waiting for transfers between devices, body(): lax.all_gather(attn_values, 'col', axis=1, tiled=True)  38.4 us
    reduce_scatter x1, waiting for transfers between devices, body(): lax.psum_scatter(value_term.reshape(-1, feature_width).astype(jnp.bfloat1...  34.6 us
    all_gather x1, waiting for transfers between devices, body(): dense_grad = lax.all_gather(output_grad, 'row', axis=1, tiled=True)[0]  30.9 us
    ppermute x3, waiting for transfers between devices, swap_dp(): return lax.ppermute(x, 'dp', [(0, 1), (1, 0)])  27.5 us
    all_gather x1, waiting for transfers between devices, body(): lax.all_gather(attn_keys, 'col', axis=1, tiled=True)  27 us
    reduce_scatter x1, waiting for transfers between devices, body(): lax.psum_scatter(key_term.reshape(-1, feature_width).astype(jnp.bfloat16)...  26.8 us
    all_gather x1, waiting for transfers between devices, body(): lax.all_gather(jnp.concatenate([output_grad, grad_other], axis=0), 'row',...  23.4 us
  transfers between devices with their start and end apart: 11, of which 9 were waited for; matrix products, arithmetic and copies ran while one was open for 13% of the time, Pallas kernels for 0%

commit v1 on v0

--- a/solution.py
+++ b/solution.py
@@ -4,6 +4,25 @@
 from jax.sharding import PartitionSpec as P
 
 DH = 128
+
+
+def gather_around(x, axis, dim):
+    size, here, rows = (lax.axis_size(axis), lax.axis_index(axis), x.shape[dim])
+    right = [(i, (i + 1) % size) for i in range(size)]
+    behind = [(i, (i - 1) % size) for i in range(size)]
+    out = jnp.zeros((*x.shape[:dim], size * rows, *x.shape[dim + 1 :]), x.dtype)
+    out = lax.dynamic_update_slice_in_dim(out, x, here * rows, axis=dim)
+    from_left = from_right = x
+    middle = size // 2
+    for hop in range(1, middle + 1):
+        from_left = lax.ppermute(from_left, axis, right)
+        out = lax.dynamic_update_slice_in_dim(out, from_left, (here - hop) % size * rows, axis=dim)
+        if hop < size - middle:
+            from_right = lax.ppermute(from_right, axis, behind)
+            out = lax.dynamic_update_slice_in_dim(
+                out, from_right, (here + hop) % size * rows, axis=dim
+            )
+    return out
 
 
 def contract_rows(left, right):
@@ -25,7 +44,7 @@
     patch_other = swap_dp(lax.all_gather(patches, "col", axis=1, tiled=True))
     every_key, every_value, every_patch = (
         lax.all_gather(attn_keys, "col", axis=1, tiled=True),
-        lax.all_gather(attn_values, "col", axis=1, tiled=True),
+        gather_around(attn_values, "col", 1),
         lax.all_gather(patches, "col", axis=1, tiled=True),
     )
     local_query = queries[0].reshape(local_rows, head_count, DH)

time: 367 us -> 355 us (0.967)
  waiting for transfers between devices: 267 us -> 237 us
  starting transfers between devices: 3.94 us -> 17.2 us
  local copies, waits for them, and re-layouts: 11.8 us -> 16.1 us
    all_gather x1 -> x0, waiting for transfers between devices: 38.4 us -> none  [body(): lax.all_gather(attn_values, 'col', axis=1, tiled=True)]
    ppermute x0 -> x3, waiting for transfers between devices: none -> 37.6 us  [the longest x2 31.7 us: gather_around(): from_left = lax.ppermute(from_left, axis, right)]
    all_gather x1, waiting for transfers between devices: 27 us -> 0.02 us  [body(): lax.all_gather(attn_keys, 'col', axis=1, tiled=True)]
    ppermute x0 -> x3, starting transfers between devices: none -> 13.4 us  [the longest x2 11.1 us: gather_around(): from_left = lax.ppermute(from_left, axis, right)]
  transfers between devices with their start and end apart: 11 -> 13, of which waited for: 9 -> 10; matrix products, arithmetic and copies ran while one was open for 13% -> 14% of each run, Pallas kernels for 0% -> 0%
where the time goes in v1:
time: 355 us
  waiting for transfers between devices  237 us (67%)
  matrix products  45.3 us (13%)
  starting transfers between devices  17.2 us (5%)
  local copies, waits for them, and re-layouts  16.1 us (5%)
  blocking collectives  14.5 us (4%)
  between operations  14.4 us (4%)
  other arithmetic  9.82 us (3%)
    reduce_scatter x1, waiting for transfers between devices, body(): lax.psum_scatter(lax.dot_general(dense_grad, out_weight, (((1,), (1,)), (...  55 us
    reduce_scatter x1, waiting for transfers between devices, body(): lax.psum_scatter(value_term.reshape(-1, feature_width).astype(jnp.bfloat1...  34.7 us
    ppermute x2, waiting for transfers between devices, gather_around(): from_left = lax.ppermute(from_left, axis, right)  31.7 us
    all_gather x1, waiting for transfers between devices, body(): dense_grad = lax.all_gather(output_grad, 'row', axis=1, tiled=True)[0]  30.9 us
    ppermute x3, waiting for transfers between devices, swap_dp(): return lax.ppermute(x, 'dp', [(0, 1), (1, 0)])  27.6 us
    reduce_scatter x1, waiting for transfers between devices, body(): lax.psum_scatter(key_term.reshape(-1, feature_width).astype(jnp.bfloat16)...  26.6 us
    all_gather x1, waiting for transfers between devices, body(): lax.all_gather(jnp.concatenate([output_grad, grad_other], axis=0), 'row',...  24 us
    dot_general x1, matrix products, body(): lax.dot_general(out_pair, grad_pair, (((0, 1), (0, 1)), ((), ())), prefer...  16.3 us
  transfers between devices with their start and end apart: 13, of which 10 were waited for; matrix products, arithmetic and copies ran while one was open for 14% of the time, Pallas kernels for 0%

profile of v1, /device:TPU:0, one launch (start us, length us, event | category | flops | bytes accessed | tf_op | source)
XLA Modules:
  0.0 354.6 jit_solution(14212232972553949455)
XLA Ops:
  9.9 30.9 %all-gather.7.cloned.1.call-done = bf16[1,512,3072]{2,1,0:T(8,128)(2,1)} async-done(((bf16[1,128,3072]{2,1,0:T(8,128)(2,1)}), bf16[1,512,3072]{2,1,0:T(8,128)(2,1)}) %all-gather.7.cloned.1.call-update) | async-done | bytes 3145744 | tf_op jit(solution)/shard_map/all_gather | solution.py:64
  40.8 10.6 %fusion.3 = f32[512,1536]{1,0:T(8,128)} fusion(bf16[1536,3072]{1,0:T(8,128)(2,1)} %param.10, bf16[1,512,3072]{2,1,0:T(8,128)(2,1)} %all-gather.7.cloned.1.call-done), kind=kOutput, calls=%fused_computation.5 | convolution fusion | flops 4831838208 | bytes 15728640 | tf_op jit(solution)/shard_map/dot_general | solution.py:66
  53.9 2.3 collective-permute-start.1
  57.0 17.6 %collective-permute-done = bf16[1,128,1536]{2,1,0:T(8,128)(2,1)S(1)} collective-permute-done((bf16[1,128,1536]{2,1,0:T(8,128)(2,1)S(1)}, bf16[1,128,1536]{2,1,0:T(8,128)(2,1)S(1)}, u32[]{:S(2)}, u32[]{:S(2)}) %collective-permute-start) | collective-permute-done | bytes 393248 | tf_op jit(solution)/shard_map/ppermute | solution.py:18
  74.8 9.6 %collective-permute-start.2 = (bf16[1,128,1536]{2,1,0:T(8,128)(2,1)S(1)}, bf16[1,128,1536]{2,1,0:T(8,128)(2,1)}, u32[]{:S(2)}, u32[]{:S(2)}) collective-permute-start(bf16[1,128,1536]{2,1,0:T(8,128)(2,1)S(1)} %collective-permute-done), channel_id=1, source_target_pairs={{0,1},{1,2},{2,3},{3,0},{4,5},{5,6},{6,7},{7,4},{8,9},{9,10},{10,1... | collective-permute-start | bytes 1179656 | tf_op jit(solution)/shard_map/ppermute | solution.py:18
  84.4 5.9 %collective-permute-done.1 = bf16[1,128,1536]{2,1,0:T(8,128)(2,1)} collective-permute-done((bf16[1,128,1536]{2,1,0:T(8,128)(2,1)S(1)}, bf16[1,128,1536]{2,1,0:T(8,128)(2,1)}, u32[]{:S(2)}, u32[]{:S(2)}) %collective-permute-start.1) | collective-permute-done | bytes 393248 | tf_op jit(solution)/shard_map/ppermute | solution.py:21
  91.7 14.1 %collective-permute-done.2 = bf16[1,128,1536]{2,1,0:T(8,128)(2,1)} collective-permute-done((bf16[1,128,1536]{2,1,0:T(8,128)(2,1)S(1)}, bf16[1,128,1536]{2,1,0:T(8,128)(2,1)}, u32[]{:S(2)}, u32[]{:S(2)}) %collective-permute-start.2) | collective-permute-done | bytes 393248 | tf_op jit(solution)/shard_map/ppermute | solution.py:18
  107.2 2.6 multiply_reduce_fusion
  111.4 55.0 %reduce-scatter.4.cloned.1.call-done = f32[128,1536]{1,0:T(8,128)} async-done(((f32[512,1536]{1,0:T(8,128)}), f32[128,1536]{1,0:T(8,128)}) %reduce-scatter.4.cloned.1.call-update) | async-done | bytes 786448 | tf_op jit(solution)/shard_map/reduce_scatter | solution.py:65
  172.5 17.9 %collective-permute-done.4 = bf16[1,128,3072]{2,1,0:T(8,128)(2,1)S(1)} collective-permute-done((bf16[1,128,3072]{2,1,0:T(8,128)(2,1)}, bf16[1,128,3072]{2,1,0:T(8,128)(2,1)S(1)}, u32[]{:S(2)}, u32[]{:S(2)}) %collective-permute-start.4) | collective-permute-done | bytes 786464 | tf_op jit(solution)/shard_map/ppermute | solution.py:35
  190.3 2.5 pad_maximum_fusion
  192.9 2.1 multiply_convert_fusion.1
  196.7 2.6 copy.36
  201.1 2.6 copy.37
  204.6 14.5 %all_gather.20 = bf16[1,512,364]{1,2,0:T(8,128)(2,1)S(1)} all-gather(bf16[1,128,364]{1,2,0:T(8,128)(2,1)S(1)} %copy-done.6), channel_id=1, replica_groups=mesh['dp'=2,'row'=4,'col'=4] {'col'}, dimensions={1}, use_global_device_ids=true | all-gather | bytes 465920 | tf_op jit(solution)/shard_map/all_gather | solution.py:48
  221.1 9.8 %collective-permute-done.5 = bf16[1,512,364]{1,2,0:T(8,128)(2,1)} collective-permute-done((bf16[1,512,364]{1,2,0:T(8,128)(2,1)S(1)}, bf16[1,512,364]{1,2,0:T(8,128)(2,1)}, u32[]{:S(2)}, u32[]{:S(2)}) %collective-permute-start.5) | collective-permute-done | bytes 372768 | tf_op jit(solution)/shard_map/ppermute | solution.py:35
  230.9 24.0 %all-gather.11.cloned.1.call-done = bf16[2,512,3072]{2,1,0:T(8,128)(2,1)} async-done(((bf16[2,128,3072]{2,1,0:T(8,128)(2,1)}), bf16[2,512,3072]{2,1,0:T(8,128)(2,1)}) %all-gather.11.cloned.1.call-update) | async-done | bytes 6291472 | tf_op jit(solution)/shard_map/all_gather | solution.py:108
  254.8 7.5 %convolution_bitcast_fusion.1 = f32[364,3072]{1,0:T(8,128)} fusion(bf16[2,512,3072]{2,1,0:T(8,128)(2,1)} %all-gather.11.cloned.1.call-done, bf16[1,512,364]{1,2,0:T(8,128)(2,1)} %collective-permute-done.5, bf16[1,512,364]{1,2,0:T(8,128)(2,1)S(1)} %all_gather.20), kind=kOutput, calls=%fused_computation.1 | convolution fusion | flops 2290462720 | bytes 11509760 | tf_op jit(solution)/shard_map/dot_general | solution.py:115
  263.8 2.4 copy.38
  266.2 26.6 %reduce-scatter.6.cloned.1.call-done = bf16[128,1536]{1,0:T(8,128)(2,1)} async-done(((bf16[512,1536]{1,0:T(8,128)(2,1)}), bf16[128,1536]{1,0:T(8,128)(2,1)}) %reduce-scatter.6.cloned.1.call-update) | async-done | bytes 393232 | tf_op jit(solution)/shard_map/reduce_scatter | solution.py:94
  292.9 2.0 bitcast_convert_fusion.1
  294.8 34.7 %reduce-scatter.8.cloned.1.call-done = bf16[128,1536]{1,0:T(8,128)(2,1)} async-done(((bf16[512,1536]{1,0:T(8,128)(2,1)}), bf16[128,1536]{1,0:T(8,128)(2,1)}) %reduce-scatter.8.cloned.1.call-update) | async-done | bytes 393232 | tf_op jit(solution)/shard_map/reduce_scatter | solution.py:100
  329.5 2.0 bitcast_convert_fusion
  331.5 16.3 %convolution_bitcast_fusion = f32[1536,3072]{1,0:T(8,128)} fusion(bf16[2,512,3072]{2,1,0:T(8,128)(2,1)} %all-gather.11.cloned.1.call-done, bf16[1,512,1536]{1,2,0:T(8,128)(2,1)} %collective-permute-done.3, bf16[1,512,1536]{1,2,0:T(8,128)(2,1)S(1)} %copy-done.7), kind=kOutput, calls=%fused_computation | convolution fusion | flops 9665249280 | bytes 28311552 | tf_op jit(solution)/shard_map/dot_general | solution.py:112
  (57 shorter events, 24.3 us)
Async XLA Ops:
  7.2 33.7 %all-gather.7.cloned.1.call-start = ((), (), s32[]{:S(2)}) async-start(), calls=%async_computation.4 | async-start | bytes 3932160 | tf_op jit(solution)/shard_map/all_gather | solution.py:64
  7.9 99.3 %all-gather.5.cloned.1.call-start = ((), (), s32[]{:S(2)}) async-start(), calls=%async_computation.3 | async-start | bytes 1966080 | tf_op jit(solution)/shard_map/all_gather | solution.py:46
  9.9 156.5 %reduce-scatter.4.cloned.1.call-start = ((), (), s32[]{:S(2)}) async-start(), calls=%async_computation.5 | async-start | bytes 3932160 | tf_op jit(solution)/shard_map/reduce_scatter | solution.py:65
  51.4 1.0 copy-start.5
  51.4 5.1 %copy-start.4 = (bf16[1,128,1536]{2,1,0:T(8,128)(2,1)S(1)}, bf16[1,128,1536]{2,1,0:T(8,128)(2,1)}, u32[]{:S(2)}) copy-start(bf16[1,128,1536]{2,1,0:T(8,128)(2,1)} %param.7) | copy-start | bytes 1179652
  51.4 169.2 %all-gather.9.cloned.1.call-start = ((), (), s32[]{:S(2)}) async-start(), calls=%async_computation.8 | async-start | bytes 1966080 | tf_op jit(solution)/shard_map/all_gather | solution.py:85
  52.4 22.2 %collective-permute-start = (bf16[1,128,1536]{2,1,0:T(8,128)(2,1)S(1)}, bf16[1,128,1536]{2,1,0:T(8,128)(2,1)S(1)}, u32[]{:S(2)}, u32[]{:S(2)}) collective-permute-start(bf16[1,128,1536]{2,1,0:T(8,128)(2,1)S(1)} %copy-done.5), channel_id=1, source_target_pairs={{0,1},{1,2},{2,3},{3,0},{4,5},{5,6},{6,7},{7,4},{8,9},{9,10},{10,1... | collective-permute-start | bytes 1179656 | tf_op jit(solution)/shard_map/ppermute | solution.py:18
  53.9 36.4 %collective-permute-start.1 = (bf16[1,128,1536]{2,1,0:T(8,128)(2,1)S(1)}, bf16[1,128,1536]{2,1,0:T(8,128)(2,1)}, u32[]{:S(2)}, u32[]{:S(2)}) collective-permute-start(bf16[1,128,1536]{2,1,0:T(8,128)(2,1)S(1)} %copy-done.5), channel_id=1, source_target_pairs={{0,3},{1,0},{2,1},{3,2},{4,7},{5,4},{6,5},{7,6},{8,11},{9,8},{10,9... | collective-permute-start | bytes 1179656 | tf_op jit(solution)/shard_map/ppermute | solution.py:21
  56.8 50.5 %copy-start.2 = (bf16[1,128,1536]{1,2,0:T(8,128)(2,1)}, bf16[1,128,1536]{1,2,0:T(8,128)(2,1)S(1)}, u32[]{:S(2)}) copy-start(bf16[1,128,1536]{1,2,0:T(8,128)(2,1)S(1)} %copy.25) | copy-start | bytes 1179652
  74.8 31.0 %collective-permute-start.2 = (bf16[1,128,1536]{2,1,0:T(8,128)(2,1)S(1)}, bf16[1,128,1536]{2,1,0:T(8,128)(2,1)}, u32[]{:S(2)}, u32[]{:S(2)}) collective-permute-start(bf16[1,128,1536]{2,1,0:T(8,128)(2,1)S(1)} %collective-permute-done), channel_id=1, source_target_pairs={{0,1},{1,2},{2,3},{3,0},{4,5},{5,6},{6,7},{7,4},{8,9},{9,10},{10,1... | collective-permute-start | bytes 1179656 | tf_op jit(solution)/shard_map/ppermute | solution.py:18
  107.2 62.4 %copy-start = (bf16[1,512,1536]{1,2,0:T(8,128)(2,1)}, bf16[1,512,1536]{1,2,0:T(8,128)(2,1)S(1)}, u32[]{:S(2)}) copy-start(bf16[1,512,1536]{1,2,0:T(8,128)(2,1)S(1)} %constant_dynamic-update-slice_fusion) | copy-start | bytes 4718596
  170.9 83.9 %all-gather.11.cloned.1.call-start = ((), (), s32[]{:S(2)}) async-start(), calls=%async_computation.9 | async-start | bytes 7864320 | tf_op jit(solution)/shard_map/all_gather | solution.py:108
  171.0 19.4 %collective-permute-start.4 = (bf16[1,128,3072]{2,1,0:T(8,128)(2,1)}, bf16[1,128,3072]{2,1,0:T(8,128)(2,1)S(1)}, u32[]{:S(2)}, u32[]{:S(2)}) collective-permute-start(bf16[1,128,3072]{2,1,0:T(8,128)(2,1)} %param.11), channel_id=1, source_target_pairs={{0,16},{16,0},{1,17},{17,1},{2,18},{18,2},{3,19},{19,3},{4,20},{20... | collective-permute-start | bytes 2359304 | tf_op jit(solution)/shard_map/ppermute | solution.py:35
  192.8 100.0 %reduce-scatter.6.cloned.1.call-start = ((), (), s32[]{:S(2)}) async-start(), calls=%async_computation.6 | async-start | bytes 1966080 | tf_op jit(solution)/shard_map/reduce_scatter | solution.py:94
  192.9 2.1 copy-start.3
  199.3 130.2 %reduce-scatter.8.cloned.1.call-start = ((), (), s32[]{:S(2)}) async-start(), calls=%async_computation.7 | async-start | bytes 1966080 | tf_op jit(solution)/shard_map/reduce_scatter | solution.py:100
  203.7 0.9 copy-start.6
  219.1 43.3 %copy-start.1 = (bf16[1,512,1536]{1,2,0:T(8,128)(2,1)S(1)}, bf16[1,512,1536]{1,2,0:T(8,128)(2,1)}, u32[]{:S(2)}) copy-start(bf16[1,512,1536]{1,2,0:T(8,128)(2,1)} %all-gather.5.cloned.1.call-done) | copy-start | bytes 4718596
  219.1 11.8 %collective-permute-start.5 = (bf16[1,512,364]{1,2,0:T(8,128)(2,1)S(1)}, bf16[1,512,364]{1,2,0:T(8,128)(2,1)}, u32[]{:S(2)}, u32[]{:S(2)}) collective-permute-start(bf16[1,512,364]{1,2,0:T(8,128)(2,1)S(1)} %all_gather.20), channel_id=1, source_target_pairs={{0,16},{16,0},{1,17},{17,1},{2,18},{18,2},{3,19},{19,3},{4,20},{20... | collective-permute-start | bytes 1118216 | tf_op jit(solution)/shard_map/ppermute | solution.py:35
  220.6 110.8 %collective-permute-start.3 = (bf16[1,512,1536]{1,2,0:T(8,128)(2,1)}, bf16[1,512,1536]{1,2,0:T(8,128)(2,1)}, u32[]{:S(2)}, u32[]{:S(2)}) collective-permute-start(bf16[1,512,1536]{1,2,0:T(8,128)(2,1)} %all-gather.9.cloned.1.call-done), channel_id=1, source_target_pairs={{0,16},{16,0},{1,17},{17,1},{2,18},{18,2},{3,19},{19,3},{4,20},{20... | collective-permute-start | bytes 4718600 | tf_op jit(solution)/shard_map/ppermute | solution.py:35
  263.8 67.6 %copy-start.7 = (bf16[1,512,1536]{1,2,0:T(8,128)(2,1)S(1)}, bf16[1,512,1536]{1,2,0:T(8,128)(2,1)}, u32[]{:S(2)}) copy-start(bf16[1,512,1536]{1,2,0:T(8,128)(2,1)} %all-gather.9.cloned.1.call-done) | copy-start | bytes 4718596
Sparse Core Ops, SparseCore 0:
  9.6 31.2 all-gather.6
  43.0 58.8 all-gather.4
  104.7 61.6 reduce-scatter.3
  171.0 37.7 all-gather.8
  210.2 44.5 all-gather.10
  257.6 35.2 reduce-scatter.5
  295.2 34.2 reduce-scatter.7
